TPU v7x, 256 devices: a whole 4x4x8 slice. The times are simulated.
256 devices in a mesh: seq: 64 (over y_lo, x, z), fsdp: 4 (over y_hi, core).
Axes of the slice: x: 4, y: 4 (y_hi: 2, y_lo: 2; y = y_hi * 2 + y_lo), z: 8, core: 2. Of those that a mesh axis runs over, the one named last changes fastest.
Arguments:
- inputs: bfloat16 [4, 16384, 1536], P(None, ('seq', 'fsdp')), may hold values from -6 to 6
- cotangent: bfloat16 [4, 16384, 1536], P(None, ('seq', 'fsdp')), may hold values from -24 to 24
- dilated_kernel_weight: bfloat16 [1536, 3, 768], P('seq', None, 'fsdp'), may hold values from -0.09375 to 0.09375
- point_weight: bfloat16 [1536, 768], P('seq', 'fsdp'), may hold values from -0.21875 to 0.21875
Outputs:
- outputs: bfloat16 [4, 16384, 1536], P(None, ('seq', 'fsdp'))
- grad_inputs: bfloat16 [4, 16384, 1536], P(None, ('seq', 'fsdp'))
- grad_conv: float32 [1536, 3, 768], P('seq', None, 'fsdp')
- grad_point: float32 [1536, 768], P('seq', 'fsdp')
All inputs are finite; a program needn't handle non-finite values.
Results may differ from a plain program's by a relative error of at most 0.0053.
Values may be sent and summed in bfloat16 or wider, within the bound.
No kernel may reach another device: no remote copies, remote signals or barrier semaphores. Data moves between devices by JAX's collectives and lax.ppermute only.
A program may use at most 128 MiB of HBM per device.

v0:
```python
import math
import jax
import jax.numpy as jnp
from jax import lax
from jax.sharding import PartitionSpec as P


def shifted(x, axis, by):
    peers = lax.axis_size(axis)
    pairs = [(i, i + by) for i in range(peers) if 0 <= i + by < peers]
    return lax.ppermute(x, axis, pairs)


def gelu_value(v):
    return 0.5 * v * (1.0 + lax.erf(v * (1.0 / math.sqrt(2.0))))


def gelu_slope(v):
    return 0.5 * (1.0 + lax.erf(v * (1.0 / math.sqrt(2.0)))) + v * jnp.exp(-0.5 * v * v) * (
        1.0 / math.sqrt(2.0 * math.pi)
    )


def contract_rows(left, right):
    return lax.dot_general(
        left, right, (((0,), (0,)), ((), ())), preferred_element_type=jnp.float32
    )


def body(inputs, cotangent, dilated_kernel_weight, point_weight):
    seqs, bins, kernel_width = inputs.shape
    rows_all = seqs * bins * lax.axis_size("seq") * lax.axis_size("fsdp")
    norm_factor = 1.0 / math.sqrt(rows_all)
    part_conv, part_point = (
        lax.all_gather(dilated_kernel_weight, "seq", axis=0, tiled=True),
        lax.all_gather(point_weight, "seq", axis=0, tiled=True),
    )
    full_conv, full_point = (
        lax.all_gather(part_conv, "fsdp", axis=2, tiled=True),
        lax.all_gather(part_point, "fsdp", axis=1, tiled=True),
    )
    half_kernel_span = full_point.shape[1]
    x = inputs.astype(jnp.float32)
    scale = lax.rsqrt(jnp.mean(x * x, axis=-1, keepdims=True) + 1e-06)
    normed = x * scale
    input_activations = gelu_value(normed).astype(jnp.bfloat16)
    flat_acts = input_activations.reshape(-1, kernel_width)
    acts_back = shifted(input_activations, ("seq", "fsdp"), 2)
    acts_ahead = shifted(input_activations, ("seq", "fsdp"), -2)
    hidden_state = jnp.dot(flat_acts, full_conv[:, 1, :], preferred_element_type=jnp.float32)
    hidden_state = hidden_state + jnp.dot(
        acts_back.reshape(-1, kernel_width), full_conv[:, 0, :], preferred_element_type=jnp.float32
    )
    hidden_state = hidden_state + jnp.dot(
        acts_ahead.reshape(-1, kernel_width), full_conv[:, 2, :], preferred_element_type=jnp.float32
    )
    mid = gelu_value(hidden_state).astype(jnp.bfloat16)
    mixed = lax.dot_general(
        mid, full_point, (((1,), (1,)), ((), ())), preferred_element_type=jnp.float32
    )
    outputs = (
        (x.reshape(-1, kernel_width) + mixed).astype(jnp.bfloat16).reshape(seqs, bins, kernel_width)
    )
    flat_cot = cotangent.reshape(-1, kernel_width)
    back_mid = jnp.dot(flat_cot, full_point, preferred_element_type=jnp.float32)
    hidden_state_gradient = (
        (back_mid * gelu_slope(hidden_state))
        .astype(jnp.bfloat16)
        .reshape(seqs, bins, half_kernel_span)
    )
    grad_later = shifted(hidden_state_gradient, ("seq", "fsdp"), -2)
    grad_earlier = shifted(hidden_state_gradient, ("seq", "fsdp"), 2)
    stacked_tap_inputs = jnp.concatenate(
        [grad_later, hidden_state_gradient, grad_earlier], axis=-1
    ).reshape(-1, 3 * half_kernel_span)
    grad_acts = lax.dot_general(
        stacked_tap_inputs,
        full_conv.reshape(kernel_width, 3 * half_kernel_span),
        (((1,), (1,)), ((), ())),
        preferred_element_type=jnp.float32,
    )
    grad_normed = grad_acts.reshape(seqs, bins, kernel_width) * gelu_slope(normed)
    inner = jnp.mean(grad_normed * x, axis=-1, keepdims=True)
    grad_inputs = (
        cotangent.astype(jnp.float32) + scale * (grad_normed - x * scale * scale * inner)
    ).astype(jnp.bfloat16)
    conv_part = contract_rows(flat_acts, stacked_tap_inputs)
    point_part = contract_rows(flat_cot, mid)
    summed = lax.psum_scatter(
        jnp.concatenate([conv_part, point_part], axis=1).reshape(
            dilated_kernel_weight.shape[0] * lax.axis_size("seq"), 4, half_kernel_span
        ),
        "seq",
        scatter_dimension=0,
        tiled=True,
    )
    reduced = lax.psum_scatter(summed, "fsdp", scatter_dimension=2, tiled=True)
    grad_conv = reduced[:, 0:3, :] * norm_factor
    grad_point = reduced[:, 3, :] * norm_factor
    return (outputs, grad_inputs, grad_conv, grad_point)


def solution(mesh):
    return jax.shard_map(
        body,
        mesh=mesh,
        in_specs=(
            P(None, ("seq", "fsdp"), None),
            P(None, ("seq", "fsdp"), None),
            P("seq", None, "fsdp"),
            P("seq", "fsdp"),
        ),
        out_specs=(
            P(None, ("seq", "fsdp"), None),
            P(None, ("seq", "fsdp"), None),
            P("seq", None, "fsdp"),
            P("seq", "fsdp"),
        ),
        check_vma=False,
    )
```

profile of v0, /device:TPU:1, one launch (start us, length us, event | category | flops | bytes accessed | tf_op | source)
XLA Modules:
  0.0 964.2 jit_solution(17117318091418794399)
XLA Ops:
  7.2 0.7 all-gather.4.cloned.1.call-update
  7.9 258.9 %all-gather.4.cloned.1.call-done = bf16[1536,3,192]{2,0,1:T(8,128)(2,1)} async-done(((bf16[24,3,192]{2,0,1:T(8,128)(2,1)}), bf16[1536,3,192]{2,0,1:T(8,128)(2,1)}) %all-gather.4.cloned.1.call-update) | async-done | bytes 1769488 | tf_op jit(solution)/shard_map/all_gather | solution.py:35
  266.8 4.0 copy.20
  271.6 132.7 %all_gather.14 = bf16[1536,192]{1,0:T(8,128)(2,1)S(1)} all-gather(bf16[24,192]{1,0:T(8,128)(2,1)S(1)} %copy-done.3), channel_id=1, replica_groups=mesh['seq'=64,'fsdp'=4] {'seq'}, dimensions={0}, use_global_device_ids=true | all-gather | bytes 599040 | tf_op jit(solution)/shard_map/all_gather | solution.py:36
  404.2 1.1 copy.21
  406.1 1.3 collective-permute-start.1
  407.4 5.5 collective-permute-start
  413.0 2.5 fusion.3
  415.4 5.4 collective-permute-done.1
  420.9 2.5 fusion.1
  423.3 5.7 collective-permute-done
  429.1 0.9 copy-done.2
  429.9 2.8 fusion.9
  432.7 82.0 %all-gather.8.cloned.1.call-done = bf16[1536,768]{0,1:T(8,128)(2,1)} async-done(((bf16[1536,192]{0,1:T(8,128)(2,1)}), bf16[1536,768]{0,1:T(8,128)(2,1)}) %all-gather.8.cloned.1.call-update) | async-done | bytes 2359312 | tf_op jit(solution)/shard_map/all_gather | solution.py:40
  514.7 2.5 fusion.15
  517.3 7.5 collective-permute-start.3
  524.7 1.3 collective-permute-start.2
  526.0 0.9 convolution_bitcast_fusion.1
  526.9 12.2 %collective-permute-done.3 = bf16[4,64,768]{2,1,0:T(8,128)(2,1)S(1)} collective-permute-done((bf16[4,64,768]{2,1,0:T(8,128)(2,1)S(1)}, bf16[4,64,768]{2,1,0:T(8,128)(2,1)S(1)}, u32[]{:S(2)}, u32[]{:S(2)}) %collective-permute-start.3) | collective-permute-done | bytes 393248 | tf_op jit(solution)/shard_map/ppermute | solution.py:11
  539.1 0.7 copy-done.4
  539.9 0.8 copy-done.6
  540.6 7.1 convolution_bitcast_fusion
  547.8 6.6 pad_maximum_fusion
  554.3 7.0 copy.34
  561.6 3.4 fusion
  565.0 6.5 multiply_reduce_fusion
  571.5 304.1 %reduce-scatter.5.cloned.1.call-done = f32[24,4,768]{2,0,1:T(8,128)} async-done(((f32[1536,4,768]{2,0,1:T(8,128)}), f32[24,4,768]{2,0,1:T(8,128)}) %reduce-scatter.5.cloned.1.call-update) | async-done | bytes 294928 | tf_op jit(solution)/shard_map/reduce_scatter | solution.py:89
  875.6 1.6 copy.28
  877.2 1.4 reshape.73
  878.7 2.8 add_convert_fusion
  881.5 73.5 %reduce-scatter.7.cloned.1.call-done = f32[192,96]{1,0:T(8,128)} async-done(((f32[768,96]{1,0:T(8,128)}), f32[192,96]{1,0:T(8,128)}) %reduce-scatter.7.cloned.1.call-update) | async-done | bytes 73744
  955.0 1.1 reshape.74
  (33 shorter events, 3.4 us)
Async XLA Ops:
  7.2 259.7 %all-gather.4.cloned.1.call-start = ((), (), s32[]{:S(2)}) async-start(), calls=%async_computation.2 | async-start | bytes 2396160 | tf_op jit(solution)/shard_map/all_gather | solution.py:35
  7.9 405.1 %all-gather.6.cloned.1.call-start = ((), (), s32[]{:S(2)}) async-start(), calls=%async_computation.3 | async-start | bytes 8847360 | tf_op jit(solution)/shard_map/all_gather | solution.py:39
  270.9 0.7 copy-start.3
  270.9 134.5 %copy-start = (bf16[4,64,1536]{2,1,0:T(8,128)(2,1)S(1)}, bf16[4,64,1536]{2,1,0:T(8,128)(2,1)}, u32[]{:S(2)}) copy-start(bf16[4,64,1536]{2,1,0:T(8,128)(2,1)} %param.4) | copy-start | bytes 2359300
  270.9 243.8 %all-gather.8.cloned.1.call-start = ((), (), s32[]{:S(2)}) async-start(), calls=%async_computation.4 | async-start | bytes 2949120 | tf_op jit(solution)/shard_map/all_gather | solution.py:40
  405.3 470.3 %reduce-scatter.5.cloned.1.call-start = ((), (), s32[]{:S(2)}) async-start(), calls=%async_computation.5 | async-start | bytes 19169280 | tf_op jit(solution)/shard_map/reduce_scatter | solution.py:89
  406.1 14.8 %collective-permute-start.1 = (bf16[4,64,1536]{2,1,0:T(8,128)(2,1)S(1)}, bf16[4,64,1536]{2,1,0:T(8,128)(2,1)S(1)}, u32[]{:S(2)}, u32[]{:S(2)}) collective-permute-start(bf16[4,64,1536]{2,1,0:T(8,128)(2,1)S(1)} %multiply_convert_fusion), channel_id=1, source_target_pairs={{2,0},{3,1},{4,2},{5,3},{6,4},{7,5},{8,6},{9,7},{10,8},{11,9},{12,... | collective-permute-start | bytes 2359304 | tf_op jit(solution)/shard_map/ppermute | solution.py:11
  407.4 21.7 %collective-permute-start = (bf16[4,64,1536]{2,1,0:T(8,128)(2,1)S(1)}, bf16[4,64,1536]{2,1,0:T(8,128)(2,1)S(1)}, u32[]{:S(2)}, u32[]{:S(2)}) collective-permute-start(bf16[4,64,1536]{2,1,0:T(8,128)(2,1)S(1)} %multiply_convert_fusion), channel_id=1, source_target_pairs={{0,2},{1,3},{2,4},{3,5},{4,6},{5,7},{6,8},{7,9},{8,10},{9,11},{10,... | collective-permute-start | bytes 2359304 | tf_op jit(solution)/shard_map/ppermute | solution.py:11
  429.0 0.9 copy-start.2
  429.9 84.8 %copy-start.1 = (bf16[4,64,1536]{2,1,0:T(8,128)(2,1)S(1)}, bf16[4,64,1536]{2,1,0:T(8,128)(2,1)}, u32[]{:S(2)}) copy-start(bf16[4,64,1536]{2,1,0:T(8,128)(2,1)} %param.5) | copy-start | bytes 2359300
  517.3 21.8 %collective-permute-start.3 = (bf16[4,64,768]{2,1,0:T(8,128)(2,1)S(1)}, bf16[4,64,768]{2,1,0:T(8,128)(2,1)S(1)}, u32[]{:S(2)}, u32[]{:S(2)}) collective-permute-start(bf16[4,64,768]{2,1,0:T(8,128)(2,1)S(1)} %bitcast.59), channel_id=1, source_target_pairs={{0,2},{1,3},{2,4},{3,5},{4,6},{5,7},{6,8},{7,9},{8,10},{9,11},{10,... | collective-permute-start | bytes 1179656 | tf_op jit(solution)/shard_map/ppermute | solution.py:11
  524.7 14.4 %collective-permute-start.2 = (bf16[4,64,768]{2,1,0:T(8,128)(2,1)S(1)}, bf16[4,64,768]{2,1,0:T(8,128)(2,1)S(1)}, u32[]{:S(2)}, u32[]{:S(2)}) collective-permute-start(bf16[4,64,768]{2,1,0:T(8,128)(2,1)S(1)} %bitcast.60), channel_id=1, source_target_pairs={{2,0},{3,1},{4,2},{5,3},{6,4},{7,5},{8,6},{9,7},{10,8},{11,9},{12,... | collective-permute-start | bytes 1179656 | tf_op jit(solution)/shard_map/ppermute | solution.py:11
  539.1 0.7 copy-start.4
  539.9 0.8 copy-start.6
  561.3 393.7 %reduce-scatter.7.cloned.1.call-start = ((), (), s32[]{:S(2)}) async-start(), calls=%async_computation.6 | async-start | bytes 491520
  561.5 3.4 copy-start.5
  561.6 3.4 copy-start.7
Sparse Core Ops, SparseCore 0:
  9.8 257.0 all-gather.3
  271.0 104.6 all-gather.5
  405.4 109.2 all-gather.7
  561.4 314.1 reduce-scatter.4
  878.8 76.1 reduce-scatter.6
where the time goes:
time: 965 us; the launch traced here: 964 us
  waiting for transfers between devices  743 us (77%)
  blocking collectives  133 us (14%)
  matrix products  28.2 us (3%)
  local copies, waits for them, and re-layouts  19.5 us (2%)
  starting transfers between devices  16 us (2%)
  between operations  13.9 us (1%)
  other arithmetic  11.3 us (1%)
    reduce_scatter x1, waiting for transfers between devices, body(): lax.psum_scatter(jnp.concatenate([conv_part, point_part], axis=1).reshape...  304 us
    all_gather x1, waiting for transfers between devices, body(): lax.all_gather(dilated_kernel_weight, 'seq', axis=0, tiled=True)  259 us
    all_gather x1, blocking collectives, body(): lax.all_gather(point_weight, 'seq', axis=0, tiled=True)  133 us
    all_gather x1, waiting for transfers between devices, body(): lax.all_gather(part_point, 'fsdp', axis=1, tiled=True)  82 us
    unnamed x6, waiting for transfers between devices  74.2 us
    ppermute x4, waiting for transfers between devices, shifted(): return lax.ppermute(x, axis, pairs)  23.4 us
  transfers between devices with their start and end apart: 9, of which 7 were waited for; matrix products, arithmetic and copies ran while one was open for 2% of the time, Pallas kernels for 0%

commit v1 on v0

--- a/solution.py
+++ b/solution.py
@@ -3,6 +3,13 @@
 import jax.numpy as jnp
 from jax import lax
 from jax.sharding import PartitionSpec as P
+
+
+def patch_shape(mat):
+    s_next = jnp.concatenate(
+        lax.all_to_all(jnp.stack([mat] * lax.psum(1, "seq"), axis=0), "seq", 0, 0), axis=0
+    )
+    return s_next
 
 
 def shifted(x, axis, by):
@@ -33,7 +40,7 @@
     norm_factor = 1.0 / math.sqrt(rows_all)
     part_conv, part_point = (
         lax.all_gather(dilated_kernel_weight, "seq", axis=0, tiled=True),
-        lax.all_gather(point_weight, "seq", axis=0, tiled=True),
+        patch_shape(point_weight),
     )
     full_conv, full_point = (
         lax.all_gather(part_conv, "fsdp", axis=2, tiled=True),

time: 965 us -> 875 us (0.907)
  blocking collectives: 133 us -> 23.1 us
  waiting for transfers between devices: 743 us -> 768 us
    all_gather x1 -> x0, blocking collectives: 133 us -> none  [body(): lax.all_gather(point_weight, 'seq', axis=0, tiled=True)]
    all_gather x1, waiting for transfers between devices: 0.02 us -> 84.8 us  [body(): lax.all_gather(part_conv, 'fsdp', axis=2, tiled=True)]
    all_gather x1, waiting for transfers between devices: 82 us -> 29 us  [body(): lax.all_gather(part_point, 'fsdp', axis=1, tiled=True)]
    all_to_all x0 -> x1, blocking collectives: none -> 23.1 us  [patch_shape(): lax.all_to_all(jnp.stack([mat] * lax.psum(1, 'seq'), axis=0), 'seq', 0, 0)]
  transfers between devices with their start and end apart: 9 -> 9, of which waited for: 7 -> 6; matrix products, arithmetic and copies ran while one was open for 2% -> 3% of each run, Pallas kernels for 0% -> 0%
where the time goes in v1:
time: 875 us; the launch traced here: 874 us
  waiting for transfers between devices  768 us (88%)
  matrix products  28.2 us (3%)
  blocking collectives  23.1 us (3%)
  local copies, waits for them, and re-layouts  19.5 us (2%)
  between operations  14 us (2%)
  other arithmetic  11.3 us (1%)
  starting transfers between devices  10.5 us (1%)
    reduce_scatter x1, waiting for transfers between devices, body(): lax.psum_scatter(jnp.concatenate([conv_part, point_part], axis=1).reshape...  306 us
    all_gather x1, waiting for transfers between devices, body(): lax.all_gather(dilated_kernel_weight, 'seq', axis=0, tiled=True)  259 us
    all_gather x1, waiting for transfers between devices, body(): lax.all_gather(part_conv, 'fsdp', axis=2, tiled=True)  84.8 us
    unnamed x6, waiting for transfers between devices  74.6 us
    all_gather x1, waiting for transfers between devices, body(): lax.all_gather(part_point, 'fsdp', axis=1, tiled=True)  29 us
    all_to_all x1, blocking collectives, patch_shape(): lax.all_to_all(jnp.stack([mat] * lax.psum(1, 'seq'), axis=0), 'seq', 0, 0)  23.1 us
  transfers between devices with their start and end apart: 9, of which 6 were waited for; matrix products, arithmetic and copies ran while one was open for 3% of the time, Pallas kernels for 0%

profile of v1, /device:TPU:1, one launch (start us, length us, event | category | flops | bytes accessed | tf_op | source)
XLA Modules:
  0.0 874.4 jit_solution(5996032466140178739)
XLA Ops:
  7.2 0.7 all-gather.4.cloned.1.call-update
  7.9 258.9 %all-gather.4.cloned.1.call-done = bf16[1536,3,192]{2,0,1:T(8,128)(2,1)} async-done(((bf16[24,3,192]{2,0,1:T(8,128)(2,1)}), bf16[1536,3,192]{2,0,1:T(8,128)(2,1)}) %all-gather.4.cloned.1.call-update) | async-done | bytes 1769488 | tf_op jit(solution)/shard_map/all_gather | solution.py:42
  266.8 4.0 copy.20
  271.6 23.1 %all_to_all.5 = bf16[64,24,192]{2,1,0:T(8,128)(2,1)S(1)} all-to-all(bf16[64,24,192]{2,1,0:T(8,128)(2,1)S(1)} %stack.2), channel_id=1, replica_groups=mesh['seq'=64,'fsdp'=4] {'seq'}, dimensions={0} | all-to-all | bytes 1179648 | tf_op jit(solution)/shard_map/all_to_all | solution.py:10
  294.7 1.1 copy.21
  296.6 1.3 collective-permute-start.1
  297.9 5.5 collective-permute-start
  303.4 84.8 %all-gather.6.cloned.1.call-done = bf16[1536,3,768]{0,2,1:T(8,128)(2,1)} async-done(((bf16[1536,3,192]{0,2,1:T(8,128)(2,1)}), bf16[1536,3,768]{0,2,1:T(8,128)(2,1)}) %all-gather.6.cloned.1.call-update) | async-done | bytes 7077904 | tf_op jit(solution)/shard_map/all_gather | solution.py:46
  388.2 2.5 fusion.3
  390.7 2.5 fusion.1
  393.2 0.9 copy-done.2
  394.0 2.8 fusion.9
  396.8 29.0 %all-gather.8.cloned.1.call-done = bf16[1536,768]{0,1:T(8,128)(2,1)} async-done(((bf16[1536,192]{0,1:T(8,128)(2,1)}), bf16[1536,768]{0,1:T(8,128)(2,1)}) %all-gather.8.cloned.1.call-update) | async-done | bytes 2359312 | tf_op jit(solution)/shard_map/all_gather | solution.py:47
  425.8 2.5 fusion.15
  428.4 2.0 collective-permute-start.3
  430.4 1.3 collective-permute-start.2
  431.7 0.9 convolution_bitcast_fusion.1
  432.5 14.4 %collective-permute-done.3 = bf16[4,64,768]{2,1,0:T(8,128)(2,1)S(1)} collective-permute-done((bf16[4,64,768]{2,1,0:T(8,128)(2,1)S(1)}, bf16[4,64,768]{2,1,0:T(8,128)(2,1)S(1)}, u32[]{:S(2)}, u32[]{:S(2)}) %collective-permute-start.3) | collective-permute-done | bytes 393248 | tf_op jit(solution)/shard_map/ppermute | solution.py:18
  446.9 0.7 copy-done.4
  447.7 0.8 copy-done.6
  448.4 7.1 convolution_bitcast_fusion
  455.6 6.6 pad_maximum_fusion
  462.1 7.0 copy.34
  469.4 3.4 fusion
  472.8 6.5 multiply_reduce_fusion
  479.3 306.1 %reduce-scatter.5.cloned.1.call-done = f32[24,4,768]{2,0,1:T(8,128)} async-done(((f32[1536,4,768]{2,0,1:T(8,128)}), f32[24,4,768]{2,0,1:T(8,128)}) %reduce-scatter.5.cloned.1.call-update) | async-done | bytes 294928 | tf_op jit(solution)/shard_map/reduce_scatter | solution.py:96
  785.5 1.6 copy.28
  787.0 1.4 reshape.79
  788.5 2.8 add_convert_fusion
  791.3 73.8 %reduce-scatter.7.cloned.1.call-done = f32[192,96]{1,0:T(8,128)} async-done(((f32[768,96]{1,0:T(8,128)}), f32[192,96]{1,0:T(8,128)}) %reduce-scatter.7.cloned.1.call-update) | async-done | bytes 73744
  865.1 1.1 reshape.80
  866.5 0.7 broadcast_multiply_fusion
  (34 shorter events, 2.8 us)
Async XLA Ops:
  7.2 259.7 %all-gather.4.cloned.1.call-start = ((), (), s32[]{:S(2)}) async-start(), calls=%async_computation.3 | async-start | bytes 2396160 | tf_op jit(solution)/shard_map/all_gather | solution.py:42
  7.9 380.3 %all-gather.6.cloned.1.call-start = ((), (), s32[]{:S(2)}) async-start(), calls=%async_computation.4 | async-start | bytes 8847360 | tf_op jit(solution)/shard_map/all_gather | solution.py:46
  270.9 0.7 copy-start.3
  270.9 155.0 %all-gather.8.cloned.1.call-start = ((), (), s32[]{:S(2)}) async-start(), calls=%async_computation.5 | async-start | bytes 2949120 | tf_op jit(solution)/shard_map/all_gather | solution.py:47
  271.6 24.3 %copy-start = (bf16[4,64,1536]{2,1,0:T(8,128)(2,1)S(1)}, bf16[4,64,1536]{2,1,0:T(8,128)(2,1)}, u32[]{:S(2)}) copy-start(bf16[4,64,1536]{2,1,0:T(8,128)(2,1)} %param.4) | copy-start | bytes 2359300
  295.8 489.6 %reduce-scatter.5.cloned.1.call-start = ((), (), s32[]{:S(2)}) async-start(), calls=%async_computation.6 | async-start | bytes 19169280 | tf_op jit(solution)/shard_map/reduce_scatter | solution.py:96
  296.6 94.1 %collective-permute-start.1 = (bf16[4,64,1536]{2,1,0:T(8,128)(2,1)S(1)}, bf16[4,64,1536]{2,1,0:T(8,128)(2,1)S(1)}, u32[]{:S(2)}, u32[]{:S(2)}) collective-permute-start(bf16[4,64,1536]{2,1,0:T(8,128)(2,1)S(1)} %multiply_convert_fusion), channel_id=1, source_target_pairs={{2,0},{3,1},{4,2},{5,3},{6,4},{7,5},{8,6},{9,7},{10,8},{11,9},{12,... | collective-permute-start | bytes 2359304 | tf_op jit(solution)/shard_map/ppermute | solution.py:18
  297.9 95.3 %collective-permute-start = (bf16[4,64,1536]{2,1,0:T(8,128)(2,1)S(1)}, bf16[4,64,1536]{2,1,0:T(8,128)(2,1)S(1)}, u32[]{:S(2)}, u32[]{:S(2)}) collective-permute-start(bf16[4,64,1536]{2,1,0:T(8,128)(2,1)S(1)} %multiply_convert_fusion), channel_id=1, source_target_pairs={{0,2},{1,3},{2,4},{3,5},{4,6},{5,7},{6,8},{7,9},{8,10},{9,11},{10,... | collective-permute-start | bytes 2359304 | tf_op jit(solution)/shard_map/ppermute | solution.py:18
  393.2 0.9 copy-start.2
  394.0 31.8 %copy-start.1 = (bf16[4,64,1536]{2,1,0:T(8,128)(2,1)S(1)}, bf16[4,64,1536]{2,1,0:T(8,128)(2,1)}, u32[]{:S(2)}) copy-start(bf16[4,64,1536]{2,1,0:T(8,128)(2,1)} %param.5) | copy-start | bytes 2359300
  428.4 18.5 %collective-permute-start.3 = (bf16[4,64,768]{2,1,0:T(8,128)(2,1)S(1)}, bf16[4,64,768]{2,1,0:T(8,128)(2,1)S(1)}, u32[]{:S(2)}, u32[]{:S(2)}) collective-permute-start(bf16[4,64,768]{2,1,0:T(8,128)(2,1)S(1)} %bitcast.61), channel_id=1, source_target_pairs={{0,2},{1,3},{2,4},{3,5},{4,6},{5,7},{6,8},{7,9},{8,10},{9,11},{10,... | collective-permute-start | bytes 1179656 | tf_op jit(solution)/shard_map/ppermute | solution.py:18
  430.4 16.6 %collective-permute-start.2 = (bf16[4,64,768]{2,1,0:T(8,128)(2,1)S(1)}, bf16[4,64,768]{2,1,0:T(8,128)(2,1)S(1)}, u32[]{:S(2)}, u32[]{:S(2)}) collective-permute-start(bf16[4,64,768]{2,1,0:T(8,128)(2,1)S(1)} %bitcast.62), channel_id=1, source_target_pairs={{2,0},{3,1},{4,2},{5,3},{6,4},{7,5},{8,6},{9,7},{10,8},{11,9},{12,... | collective-permute-start | bytes 1179656 | tf_op jit(solution)/shard_map/ppermute | solution.py:18
  446.9 0.7 copy-start.4
  447.7 0.8 copy-start.6
  469.1 396.0 %reduce-scatter.7.cloned.1.call-start = ((), (), s32[]{:S(2)}) async-start(), calls=%async_computation.7 | async-start | bytes 491520
  469.3 3.4 copy-start.5
  469.4 3.4 copy-start.7
Sparse Core Ops, SparseCore 0:
  9.8 257.0 all-gather.3
  271.0 117.1 all-gather.5
  390.6 35.2 all-gather.7
  469.2 316.1 reduce-scatter.4
  788.6 76.4 reduce-scatter.6
